TPU v7x, 128 devices: a whole 4x4x4 slice. The times are simulated.
128 devices in a mesh: row: 8 (over x, core), col: 16 (over z, y).
Axes of the slice: x: 4, y: 4, z: 4, core: 2. Of those that a mesh axis runs over, the one named last changes fastest.
Arguments:
- left_factor: float32 [23, 8, 128, 16, 16, 128], P(None, 'row', None, None, 'col'), may hold values from -5 to 5
- pick_site: int32 [23, 8, 128], P(None, 'row'), may hold values from 0 to 131071
- noise: float32 [23, 8, 128], P(None, 'row'), may hold values from 2 to 5
Outputs:
- panels: float32 [8, 16, 184, 2, 128], P('row', 'col')
All inputs are finite; a program needn't handle non-finite values.
Results may differ from a plain program's by a relative error of at most 0.000064.
Values sent between devices are 32-bit elements; how exact they have to be, the bound alone decides.
No kernel may reach another device: no remote copies, remote signals or barrier semaphores. Data moves between devices by JAX's collectives and lax.ppermute only.
A program may use at most 128 MiB of HBM per device.

v0:
```python
import jax
import jax.numpy as jnp
from jax import lax
from jax.sharding import PartitionSpec as P

GRID_Y = 64
GRID_Z = 32


LATERAL = 24.0
VERTICAL = 6.0


def spread(block, axis, owner):
    block = jnp.where(lax.axis_index(axis) == owner, block, jnp.zeros_like(block))
    return lax.psum(block, axis)


def site_coords(site_ids):
    coord_x = site_ids // (GRID_Y * GRID_Z)
    coord_y = site_ids // GRID_Z % GRID_Y
    coord_z = site_ids % GRID_Z
    return jnp.stack([coord_x, coord_y, coord_z]).astype(jnp.float32)


def matern(row_coords, col_coords):
    lengths = (LATERAL, LATERAL, VERTICAL)
    squared = jnp.zeros((row_coords.shape[1], col_coords.shape[1]), jnp.float32)
    for dim_index in range(3):
        difference = (row_coords[dim_index][:, None] - col_coords[dim_index][None, :]) / lengths[
            dim_index
        ]
        squared = squared + difference * difference
    radius = jnp.sqrt(3.0 * squared)
    return (1.0 + radius) * jnp.exp(-radius)


def times_transposed(left_mat, right_mat):
    return lax.dot_general(
        left_mat,
        right_mat,
        (((1,), (1,)), ((), ())),
        precision=lax.Precision.HIGHEST,
        preferred_element_type=jnp.float32,
    )


def lower_inverse(square):
    factor = jnp.linalg.cholesky(square)
    return jax.scipy.linalg.solve_triangular(
        factor, jnp.eye(square.shape[0], dtype=jnp.float32), lower=True
    )


def body(left_factor, pick_site, noise):
    row_blocks, _, block_width, col_blocks, _, _ = left_factor.shape
    col_count = lax.axis_size("col")
    row_share = row_blocks * block_width // col_count
    row_index = lax.axis_index("row")
    col_index = lax.axis_index("col")
    local_rows = left_factor.reshape(row_blocks * block_width, col_blocks * block_width)
    site_flat = pick_site.reshape(row_blocks * block_width)
    noise_flat = noise.reshape(row_blocks * block_width)
    offset = col_index * row_share
    my_coords = site_coords(lax.dynamic_slice_in_dim(site_flat, offset, row_share))
    my_noise = lax.dynamic_slice_in_dim(noise_flat, offset, row_share)
    head_rows = local_rows[:block_width]
    head_coords = site_coords(site_flat[:block_width])
    first_owner = (row_index == 0) & (col_index == 0)
    second_owner = (row_index == 1) & (col_index == 0)
    own_diag = jnp.diag(my_noise[:block_width])

    def terms_for(lead_rows):
        return times_transposed(local_rows, lead_rows)

    first_head, first_coords = (spread(head_rows, "row", 0), spread(head_coords, "row", 0))
    first_sums = lax.psum_scatter(terms_for(first_head), "col", scatter_dimension=0, tiled=True)
    second_head, second_coords = (spread(head_rows, "row", 1), spread(head_coords, "row", 1))
    second_sums = lax.psum_scatter(terms_for(second_head), "col", scatter_dimension=0, tiled=True)
    first_cov = matern(my_coords, first_coords) - first_sums
    first_cov = first_cov.at[:block_width].add(jnp.where(first_owner, own_diag, 0.0))
    first_diag = spread(first_cov[:block_width], ("row", "col"), 0)
    first_panel = times_transposed(first_cov, lower_inverse(first_diag))
    own_cross = first_panel[:block_width]
    second_base = matern(my_coords, second_coords) - second_sums
    second_nugget = jnp.where(second_owner, own_diag, 0.0)
    cross_rows = spread(own_cross, ("row", "col"), col_count)
    second_cov = (
        (second_base - times_transposed(first_panel, cross_rows))
        .at[:block_width]
        .add(second_nugget)
    )
    second_diag = spread(second_cov[:block_width], ("row", "col"), col_count)
    second_panel = times_transposed(second_cov, lower_inverse(second_diag))
    stacked = jnp.stack([first_panel, second_panel], axis=1)
    return stacked.reshape(1, 1, row_share, 2, block_width)


def solution(mesh):
    placed = (P(None, "row", None, None, "col", None), P(None, "row", None), P(None, "row", None))
    return jax.shard_map(
        body,
        mesh=mesh,
        in_specs=placed,
        out_specs=P("row", "col", None, None, None),
        check_vma=False,
    )
```

profile of v0, /device:TPU:4, one launch (start us, length us, event | category | flops | bytes accessed | tf_op | source)
XLA Modules:
  0.0 738.3 jit_solution(13601761181299983725)
XLA Ops:
  6.5 6.9 fusion.13
  13.5 2.3 copy_bitcast_fusion
  15.8 64.0 %all-reduce.19.cloned.1.call-done = (f32[128,2048]{1,0:T(8,128)}, f32[128,2048]{1,0:T(8,128)}) async-done(((f32[128,2048]{1,0:T(8,128)}, f32[128,2048]{1,0:T(8,128)}), (f32[128,2048]{1,0:T(8,128)}, f32[128,2048]{1,0:T(8,128)})) %all-reduce.19.cloned.1.call-update) | async-done | bytes 2097168 | tf_op jit(solution)/shard_map/psum | solution.py:16
  79.9 40.9 %fusion.6 = f32[2944,128]{0,1:T(8,128)} fusion(f32[128,2048]{1,0:T(8,128)} %get-tuple-element.37, f32[368,8,16,128]{3,2,1,0:T(8,128)} %bitcast.102), kind=kOutput, calls=%fused_computation.6 | convolution fusion | flops 9261023232 | bytes 26673152 | tf_op jit(solution)/shard_map/dot_general | solution.py:39
  120.8 40.5 %fusion.9 = f32[2944,128]{0,1:T(8,128)} fusion(f32[128,2048]{1,0:T(8,128)S(1)} %copy-done, f32[368,8,16,128]{3,2,1,0:T(8,128)} %bitcast.103), kind=kOutput, calls=%fused_computation.7 | convolution fusion | flops 9261023232 | bytes 26673152 | tf_op jit(solution)/shard_map/dot_general | solution.py:39
  161.6 0.6 dynamic-slice.16
  162.9 12.1 %all-reduce.3 = (f32[3,128]{1,0:T(4,128)S(1)}, f32[3,128]{1,0:T(4,128)S(1)}) all-reduce(f32[3,128]{1,0:T(4,128)S(1)} %get-tuple-element.59, f32[3,128]{1,0:T(4,128)S(1)} %get-tuple-element.58), channel_id=1, replica_groups=mesh['row'=8,'col'=16] {'row'}, use_global_device_ids=true, to_apply=%region_0.1 | all-reduce | flops 768 | bytes 6144 | tf_op jit(solution)/shard_map/psum | solution.py:16
  175.1 85.5 %all-reduce.17.cloned.1.call-done = (f32[2944,128]{0,1:T(8,128)}, f32[2944,128]{0,1:T(8,128)}) async-done(((f32[2944,128]{0,1:T(8,128)}, f32[2944,128]{0,1:T(8,128)}), (f32[2944,128]{0,1:T(8,128)}, f32[2944,128]{0,1:T(8,128)})) %all-reduce.17.cloned.1.call-update) | async-done | bytes 3014672
  260.6 1.1 dynamic-slice_subtract_fusion.1
  261.7 0.7 fusion.28
  262.5 138.7 %all-reduce.11.cloned.1.call-done = f32[128,128]{0,1:T(8,128)} async-done(((f32[128,128]{0,1:T(8,128)}), f32[128,128]{0,1:T(8,128)}) %all-reduce.11.cloned.1.call-update) | async-done | bytes 65552 | tf_op jit(solution)/shard_map/psum | solution.py:16
  401.2 0.9 copy.15
  402.1 0.9 fusion.25
  403.0 11.7 %cholesky.44 = f32[128,128]{1,0:T(8,128)S(1)} custom-call(f32[128,128]{1,0:T(8,128)S(1)} %fusion.25), custom_call_target="Cholesky" | custom-call | tf_op jit(solution)/shard_map/jit(cholesky)/cholesky | solution.py:49
  414.7 0.6 compare_reduce_fusion.1
  415.4 0.7 fusion.18
  416.0 9.8 %custom-call.6 = f32[1,128,128]{1,2,0:T(8,128)S(1)} custom-call(f32[1,128,128]{2,1,0:T(8,128)S(1)} %fusion.18), custom_call_target="InvertDiagBlocksLowerTriangular" | custom-call | tf_op jit(solution)/shard_map/jit(_solve_triangular)/triangular_solve | solution.py:50
  426.1 0.4 fusion.35
  426.7 0.6 broadcast_select_fusion.2
  427.3 0.3 all-reduce.15.cloned.1.call-start
  427.7 136.5 %all-reduce.13.cloned.1.call-done = f32[128,128]{0,1:T(8,128)} async-done(((f32[128,128]{0,1:T(8,128)}), f32[128,128]{0,1:T(8,128)}) %all-reduce.13.cloned.1.call-update) | async-done | bytes 65552 | tf_op jit(solution)/shard_map/psum | solution.py:16
  564.1 1.3 convolution_subtract_fusion
  565.5 0.7 fusion.26
  566.2 139.2 %all-reduce.15.cloned.1.call-done = f32[128,128]{0,1:T(8,128)} async-done(((f32[128,128]{0,1:T(8,128)}), f32[128,128]{0,1:T(8,128)}) %all-reduce.15.cloned.1.call-update) | async-done | bytes 65552 | tf_op jit(solution)/shard_map/psum | solution.py:16
  705.4 0.9 copy.19
  706.3 0.9 fusion.23
  707.1 11.7 %cholesky.55 = f32[128,128]{1,0:T(8,128)S(1)} custom-call(f32[128,128]{1,0:T(8,128)S(1)} %fusion.23), custom_call_target="Cholesky" | custom-call | tf_op jit(solution)/shard_map/jit(cholesky)/cholesky | solution.py:49
  718.9 0.6 compare_reduce_fusion
  719.5 0.7 fusion.19
  720.2 9.8 %custom-call.7 = f32[1,128,128]{1,2,0:T(8,128)S(1)} custom-call(f32[1,128,128]{2,1,0:T(8,128)S(1)} %fusion.19), custom_call_target="InvertDiagBlocksLowerTriangular" | custom-call | tf_op jit(solution)/shard_map/jit(_solve_triangular)/triangular_solve | solution.py:50
  730.3 0.4 convolution_bitcast_fusion
  730.8 0.8 copy.20
  (35 shorter events, 1.3 us)
Async XLA Ops:
  6.5 73.3 %all-reduce.19.cloned.1.call-start = ((), (), s32[]{:S(2)}) async-start(), calls=%async_computation.4 | async-start | bytes 4194304 | tf_op jit(solution)/shard_map/psum | solution.py:16
  15.8 244.8 %all-reduce.17.cloned.1.call-start = ((), (), s32[]{:S(2)}) async-start(), calls=%async_computation.3 | async-start | bytes 6029312
  79.9 40.9 %copy-start = (f32[128,2048]{1,0:T(8,128)S(1)}, f32[128,2048]{1,0:T(8,128)}, u32[]{:S(2)}) copy-start(f32[128,2048]{1,0:T(8,128)} %get-tuple-element.38) | copy-start | bytes 3145732
  79.9 81.5 %copy-start.1 = (s32[23,1,128]{2,1,0:T(1,128)S(1)}, s32[23,1,128]{2,1,0:T(1,128)}, u32[]{:S(2)}) copy-start(s32[23,1,128]{2,1,0:T(1,128)} %param.11) | copy-start | bytes 35332
  79.9 81.6 %copy-start.2 = (f32[23,1,128]{2,1,0:T(1,128)S(1)}, f32[23,1,128]{2,1,0:T(1,128)}, u32[]{:S(2)}) copy-start(f32[23,1,128]{2,1,0:T(1,128)} %param.12) | copy-start | bytes 35332
  79.9 81.7 %copy-start.3 = (u32[128]{0:T(128)S(1)}, u32[128]{0:T(128)}, u32[]{:S(2)}) copy-start(u32[128]{0:T(128)} %constant.200) | copy-start | bytes 1540
  161.3 239.8 %all-reduce.11.cloned.1.call-start = ((), (), s32[]{:S(2)}) async-start(), calls=%async_computation | async-start | bytes 131072 | tf_op jit(solution)/shard_map/psum | solution.py:16
  262.4 301.7 %all-reduce.13.cloned.1.call-start = ((), (), s32[]{:S(2)}) async-start(), calls=%async_computation.1 | async-start | bytes 131072 | tf_op jit(solution)/shard_map/psum | solution.py:16
  427.3 278.0 %all-reduce.15.cloned.1.call-start = ((), (), s32[]{:S(2)}) async-start(), calls=%async_computation.2 | async-start | bytes 131072 | tf_op jit(solution)/shard_map/psum | solution.py:16
Sparse Core Ops, SparseCore 0:
  15.9 63.8 all-reduce.18
  161.5 99.0 all-reduce.16
  265.3 135.8 all-reduce.10
  427.5 136.6 all-reduce.12
  568.7 136.5 all-reduce.14
where the time goes:
time: 746 us; the launch traced here: 738 us
  waiting for transfers between devices  564 us (76%)
  matrix products  84.2 us (11%)
  other arithmetic  57.7 us (8%)
  between operations  14.3 us (2%)
  blocking collectives  12.1 us (2%)
    psum x4, waiting for transfers between devices, spread(): return lax.psum(block, axis)  478 us
    unnamed x6, waiting for transfers between devices  85.6 us
    dot_general x5, matrix products, times_transposed(): lax.dot_general(left_mat, right_mat, (((1,), (1,)), ((), ())), precision=...  83.6 us
    another operation x6, other arithmetic, lower_inverse(): factor = jnp.linalg.cholesky(square)  24.8 us
    another operation x4, other arithmetic, lower_inverse(): jax.scipy.linalg.solve_triangular(factor, jnp.eye(square.shape[0], dtype=...  20.9 us
  transfers between devices with their start and end apart: 5, of which 5 were waited for; matrix products, arithmetic and copies ran while one was open for 0% of the time, Pallas kernels for 0%

commit v1 on v0

--- a/solution.py
+++ b/solution.py
@@ -9,11 +9,6 @@
 
 LATERAL = 24.0
 VERTICAL = 6.0
-
-
-def spread(block, axis, owner):
-    block = jnp.where(lax.axis_index(axis) == owner, block, jnp.zeros_like(block))
-    return lax.psum(block, axis)
 
 
 def site_coords(site_ids):
@@ -64,34 +59,59 @@
     offset = col_index * row_share
     my_coords = site_coords(lax.dynamic_slice_in_dim(site_flat, offset, row_share))
     my_noise = lax.dynamic_slice_in_dim(noise_flat, offset, row_share)
-    head_rows = local_rows[:block_width]
-    head_coords = site_coords(site_flat[:block_width])
     first_owner = (row_index == 0) & (col_index == 0)
     second_owner = (row_index == 1) & (col_index == 0)
     own_diag = jnp.diag(my_noise[:block_width])
 
-    def terms_for(lead_rows):
-        return times_transposed(local_rows, lead_rows)
+    head_rows = local_rows[:block_width]
+    head_info = jnp.concatenate(
+        [site_coords(site_flat[:block_width]), noise_flat[None, :block_width]], axis=0
+    )
+    is_first = row_index == 0
+    is_second = row_index == 1
+    heads = jnp.concatenate(
+        [jnp.where(is_first, head_rows, 0.0), jnp.where(is_second, head_rows, 0.0)], axis=0
+    )
+    info = jnp.concatenate(
+        [jnp.where(is_first, head_info, 0.0), jnp.where(is_second, head_info, 0.0)], axis=1
+    )
+    heads, info = lax.psum((heads, info), "row")
 
-    first_head, first_coords = (spread(head_rows, "row", 0), spread(head_coords, "row", 0))
-    first_sums = lax.psum_scatter(terms_for(first_head), "col", scatter_dimension=0, tiled=True)
-    second_head, second_coords = (spread(head_rows, "row", 1), spread(head_coords, "row", 1))
-    second_sums = lax.psum_scatter(terms_for(second_head), "col", scatter_dimension=0, tiled=True)
-    first_cov = matern(my_coords, first_coords) - first_sums
+    terms = lax.dot_general(
+        local_rows.reshape(col_count, row_share, col_blocks * block_width),
+        heads,
+        (((2,), (1,)), ((), ())),
+        precision=lax.Precision.HIGHEST,
+        preferred_element_type=jnp.float32,
+    )
+    gram = lax.psum(times_transposed(heads, heads), "col")
+    sums = lax.psum_scatter(terms, "col", scatter_dimension=0, tiled=False)
+
+    first_coords = info[:3, :block_width]
+    second_coords = info[:3, block_width:]
+    first_diag = matern(first_coords, first_coords) - gram[:block_width, :block_width]
+    first_diag = first_diag + jnp.diag(info[3, :block_width])
+    first_inverse = lower_inverse(first_diag)
+    cross_rows = times_transposed(
+        matern(second_coords, first_coords) - gram[block_width:, :block_width], first_inverse
+    )
+    second_diag = (
+        matern(second_coords, second_coords)
+        - gram[block_width:, block_width:]
+        - times_transposed(cross_rows, cross_rows)
+    )
+    second_diag = second_diag + jnp.diag(info[3, block_width:])
+    second_inverse = lower_inverse(second_diag)
+
+    first_cov = matern(my_coords, first_coords) - sums[:, :block_width]
     first_cov = first_cov.at[:block_width].add(jnp.where(first_owner, own_diag, 0.0))
-    first_diag = spread(first_cov[:block_width], ("row", "col"), 0)
-    first_panel = times_transposed(first_cov, lower_inverse(first_diag))
-    own_cross = first_panel[:block_width]
-    second_base = matern(my_coords, second_coords) - second_sums
-    second_nugget = jnp.where(second_owner, own_diag, 0.0)
-    cross_rows = spread(own_cross, ("row", "col"), col_count)
+    first_panel = times_transposed(first_cov, first_inverse)
     second_cov = (
-        (second_base - times_transposed(first_panel, cross_rows))
-        .at[:block_width]
-        .add(second_nugget)
+        (matern(my_coords, second_coords) - sums[:, block_width:])
+        - times_transposed(first_panel, cross_rows)
     )
-    second_diag = spread(second_cov[:block_width], ("row", "col"), col_count)
-    second_panel = times_transposed(second_cov, lower_inverse(second_diag))
+    second_cov = second_cov.at[:block_width].add(jnp.where(second_owner, own_diag, 0.0))
+    second_panel = times_transposed(second_cov, second_inverse)
     stacked = jnp.stack([first_panel, second_panel], axis=1)
     return stacked.reshape(1, 1, row_share, 2, block_width)
 

time: 746 us -> 293 us (0.39)
  waiting for transfers between devices: 564 us -> 81.4 us
  other arithmetic: 57.7 us -> 123 us
  matrix products: 84.2 us -> 32.1 us
  local copies, waits for them, and re-layouts: 5.72 us -> 30.6 us
    psum x4 -> x2, waiting for transfers between devices: 478 us -> 52.7 us  [the longest x1 52.7 us: body(): gram = lax.psum(times_transposed(heads, heads), 'col')]
    dot_general x5 -> x6, matrix products: 83.6 us -> 8.48 us  [times_transposed(): lax.dot_general(left_mat, right_mat, (((1,), (1,)), ((), ())), precision=...]
    unnamed x2 -> x3, other arithmetic: 0.07 us -> 66.7 us
    unnamed x6 -> x4, waiting for transfers between devices: 85.6 us -> 28.7 us
    another operation x0 -> x1, local copies, waits for them, and re-layouts: none -> 26.4 us  [body(): local_rows.reshape(col_count, row_share, col_blocks * block_width)]
    dot_general x0 -> x1, matrix products: none -> 23.1 us  [body(): lax.dot_general(local_rows.reshape(col_count, row_share, col_blocks * blo...]
  transfers between devices with their start and end apart: 5 -> 3, of which waited for: 5 -> 2; matrix products, arithmetic and copies ran while one was open for 0% -> 58% of each run, Pallas kernels for 0% -> 0%
where the time goes in v1:
time: 293 us; the launch traced here: 292 us
  other arithmetic  123 us (42%)
  waiting for transfers between devices  81.4 us (28%)
  matrix products  32.1 us (11%)
  local copies, waits for them, and re-layouts  30.6 us (10%)
  between operations  13.4 us (5%)
  blocking collectives  10.5 us (4%)
    unnamed x3, other arithmetic  66.7 us
    psum x1, waiting for transfers between devices, body(): gram = lax.psum(times_transposed(heads, heads), 'col')  52.7 us
    unnamed x4, waiting for transfers between devices  28.7 us
    another operation x1, local copies, waits for them, and re-layouts, body(): local_rows.reshape(col_count, row_share, col_blocks * block_width)  26.4 us
    another operation x6, other arithmetic, lower_inverse(): factor = jnp.linalg.cholesky(square)  24.8 us
    dot_general x1, matrix products, body(): lax.dot_general(local_rows.reshape(col_count, row_share, col_blocks * blo...  23.1 us
    another operation x4, other arithmetic, lower_inverse(): jax.scipy.linalg.solve_triangular(factor, jnp.eye(square.shape[0], dtype=...  21.1 us
    psum x1, blocking collectives, body(): heads, info = lax.psum((heads, info), 'row')  10.5 us
  transfers between devices with their start and end apart: 3, of which 2 were waited for; matrix products, arithmetic and copies ran while one was open for 58% of the time, Pallas kernels for 0%

profile of v1, /device:TPU:4, one launch (start us, length us, event | category | flops | bytes accessed | tf_op | source)
XLA Modules:
  0.0 291.6 jit_solution(3037362575774388247)
XLA Ops:
  6.5 6.9 %fusion.6 = (f32[128,16,128]{2,1,0:T(8,128)S(1)}, f32[128,16,128]{2,1,0:T(8,128)S(1)}) fusion(pred[]{:T(512)S(6)} %eq.34, f32[23,1,128,16,1,128]{5,4,3,2,1,0:T(1,128)} %param.10, pred[]{:T(512)S(6)} %eq.35), kind=kLoop, calls=%fused_computation.10 | loop fusion | flops 524288 | bytes 3145730 | tf_op jit(solution)/shard_map/jit(_where)/select_n | solution.py:73
  13.5 0.9 copy_bitcast_fusion
  14.3 1.5 pad_maximum_fusion
  15.9 0.5 broadcast.389
  16.4 66.6 %reduce.21 = f32[23,128,16,128]{3,2,1,0:T(8,128)} reduce(f32[23,1,128,16,1,128]{5,4,3,2,1,0:T(1,128)} %param.10, f32[]{:T(128)} %broadcast.389), dimensions={1,4}, to_apply=%param.10.reduce_sub_computation.3 | reduce | bytes 48234500 | tf_op args[0]
  83.0 26.4 %reshape_reshape.3 = f32[16,184,2048]{2,1,0:T(8,128)} reshape(f32[23,128,16,128]{3,2,1,0:T(8,128)} %reduce.21) | data formatting | bytes 48234496 | tf_op jit(solution)/shard_map/reshape;reshape | solution.py:81
  109.4 4.9 %fusion.60 = f32[256,256]{0,1:T(8,128)} fusion(f32[256,2048]{1,0:T(8,128)} %all-reduce.4.cloned.1.call-done), kind=kOutput, calls=%fused_computation.128 | convolution fusion | flops 1610612736 | bytes 2359296 | tf_op jit(solution)/shard_map/dot_general | solution.py:34
  114.4 0.2 reduce-scatter.4.cloned.1.call-start
  114.6 23.1 %fusion.2 = f32[16,184,256]{2,1,0:T(8,128)} fusion(f32[16,184,2048]{2,1,0:T(8,128)} %reshape_reshape.3, f32[256,2048]{1,0:T(8,128)S(1)} %copy-done), kind=kOutput, calls=%fused_computation.5 | convolution fusion | flops 18522046464 | bytes 29229056 | tf_op jit(solution)/shard_map/dot_general | solution.py:80
  137.8 0.7 copy-done.1
  138.7 10.5 %psum.21 = f32[4,256]{1,0:T(4,128)S(1)} all-reduce(f32[4,256]{1,0:T(4,128)S(1)} %pad_maximum_fusion.1), channel_id=1, replica_groups=mesh['row'=8,'col'=16] {'row'}, use_global_device_ids=true, to_apply=%region_0.1 | all-reduce | flops 1024 | bytes 8192 | tf_op jit(solution)/shard_map/psum | solution.py:78
  149.3 52.7 %all-reduce.6.cloned.1.call-done = f32[256,256]{0,1:T(8,128)} async-done(((f32[256,256]{0,1:T(8,128)}), f32[256,256]{0,1:T(8,128)}) %all-reduce.6.cloned.1.call-update) | async-done | bytes 262160 | tf_op jit(solution)/shard_map/psum | solution.py:87
  202.0 1.0 fusion.19
  203.1 1.0 fusion.23
  204.1 11.7 %cholesky.44 = f32[128,128]{1,0:T(8,128)S(1)} custom-call(f32[128,128]{1,0:T(8,128)S(1)} %fusion.23), custom_call_target="Cholesky" | custom-call | tf_op jit(solution)/shard_map/jit(cholesky)/cholesky | solution.py:44
  215.9 0.6 compare_reduce_fusion.1
  216.5 0.7 fusion.12
  217.2 9.8 %custom-call.6 = f32[1,128,128]{1,2,0:T(8,128)S(1)} custom-call(f32[1,128,128]{2,1,0:T(8,128)S(1)} %fusion.12), custom_call_target="InvertDiagBlocksLowerTriangular" | custom-call | tf_op jit(solution)/shard_map/jit(_solve_triangular)/triangular_solve | solution.py:45
  227.0 0.3 fusion.10
  227.3 1.2 fusion.18
  228.5 1.1 fusion.5
  229.7 11.7 %cholesky.55 = f32[128,128]{1,0:T(8,128)S(1)} custom-call(f32[128,128]{1,0:T(8,128)S(1)} %fusion.21), custom_call_target="Cholesky" | custom-call | tf_op jit(solution)/shard_map/jit(cholesky)/cholesky | solution.py:44
  241.5 0.6 compare_reduce_fusion
  242.1 0.7 fusion.13
  242.8 10.0 %custom-call.7 = f32[1,128,128]{1,2,0:T(8,128)S(1)} custom-call(f32[1,128,128]{2,1,0:T(8,128)S(1)} %fusion.13), custom_call_target="InvertDiagBlocksLowerTriangular" | custom-call | tf_op jit(solution)/shard_map/jit(_solve_triangular)/triangular_solve | solution.py:45
  252.8 0.3 fusion.8
  253.1 28.7 %reduce-scatter.4.cloned.1.call-done = f32[1,184,256]{2,1,0:T(8,128)} async-done(((f32[16,184,256]{2,1,0:T(8,128)}), f32[1,184,256]{2,1,0:T(8,128)}) %reduce-scatter.4.cloned.1.call-update) | async-done | bytes 188432
  281.8 1.1 copy.19
  283.0 0.4 fusion.61
  283.5 0.4 convolution_subtract_fusion
  283.9 0.4 convolution_bitcast_fusion
  284.3 0.8 copy.26
  (33 shorter events, 0.9 us)
Async XLA Ops:
  6.5 102.9 %all-reduce.4.cloned.1.call-start = ((), (), s32[]{:S(2)}) async-start(), calls=%async_computation.1 | async-start | bytes 4194304 | tf_op jit(solution)/shard_map/psum | solution.py:78
  15.8 186.2 %all-reduce.6.cloned.1.call-start = ((), (), s32[]{:S(2)}) async-start(), calls=%async_computation.2 | async-start | bytes 524288 | tf_op jit(solution)/shard_map/psum | solution.py:87
  109.4 5.2 %copy-start = (f32[256,2048]{1,0:T(8,128)S(1)}, f32[256,2048]{1,0:T(8,128)}, u32[]{:S(2)}) copy-start(f32[256,2048]{1,0:T(8,128)} %all-reduce.4.cloned.1.call-done) | copy-start | bytes 6291460
  114.4 167.4 %reduce-scatter.4.cloned.1.call-start = ((), (), s32[]{:S(2)}) async-start(), calls=%async_computation.3 | async-start | bytes 3203072
  137.7 0.7 copy-start.1
  137.7 0.7 copy-start.2
Sparse Core Ops, SparseCore 0:
  15.9 63.7 all-reduce.3
  114.5 87.4 all-reduce.5
  205.4 76.3 reduce-scatter.3

commit v2 on v1

--- a/solution.py
+++ b/solution.py
@@ -47,6 +47,15 @@
     )
 
 
+def col_sum(block):
+    count = lax.axis_size("col")
+    step = 1
+    while step < count:
+        block = block + lax.ppermute(block, "col", [(i, i ^ step) for i in range(count)])
+        step *= 2
+    return block
+
+
 def body(left_factor, pick_site, noise):
     row_blocks, _, block_width, col_blocks, _, _ = left_factor.shape
     col_count = lax.axis_size("col")
@@ -75,17 +84,14 @@
     info = jnp.concatenate(
         [jnp.where(is_first, head_info, 0.0), jnp.where(is_second, head_info, 0.0)], axis=1
     )
-    heads, info = lax.psum((heads, info), "row")
+    info_rows = jnp.zeros((8, heads.shape[1]), jnp.float32).at[:4, : 2 * block_width].set(info)
+    packed = lax.psum(jnp.concatenate([heads, info_rows], axis=0), "row")
+    heads = packed[: 2 * block_width]
+    info = packed[2 * block_width : 2 * block_width + 4, : 2 * block_width]
 
-    terms = lax.dot_general(
-        local_rows.reshape(col_count, row_share, col_blocks * block_width),
-        heads,
-        (((2,), (1,)), ((), ())),
-        precision=lax.Precision.HIGHEST,
-        preferred_element_type=jnp.float32,
-    )
-    gram = lax.psum(times_transposed(heads, heads), "col")
+    terms = times_transposed(local_rows, heads).reshape(col_count, row_share, 2 * block_width)
     sums = lax.psum_scatter(terms, "col", scatter_dimension=0, tiled=False)
+    gram = col_sum(times_transposed(heads, heads))
 
     first_coords = info[:3, :block_width]
     second_coords = info[:3, block_width:]

time: 293 us -> 229 us (0.78)
  other arithmetic: 123 us -> 55.9 us
  local copies, waits for them, and re-layouts: 30.6 us -> 7.55 us
  waiting for transfers between devices: 81.4 us -> 96.4 us
  starting transfers between devices: 0.27 us -> 10.9 us
  blocking collectives: 10.5 us -> 0 us
  matrix products: 32.1 us -> 41.3 us
    unnamed x3 -> x2, other arithmetic: 66.7 us -> 0.06 us
    ppermute x0 -> x4, waiting for transfers between devices: none -> 32.4 us  [col_sum(): lax.ppermute(block, 'col', [(i, i ^ step) for i in range(count)])]
    dot_general x6 -> x7, matrix products: 8.48 us -> 40.7 us  [times_transposed(): lax.dot_general(left_mat, right_mat, (((1,), (1,)), ((), ())), precision=...]
    unnamed x4 -> x3, waiting for transfers between devices: 28.7 us -> 0.05 us
    another operation x1 -> x0, local copies, waits for them, and re-layouts: 26.4 us -> none  [body(): local_rows.reshape(col_count, row_share, col_blocks * block_width)]
    dot_general x1 -> x0, matrix products: 23.1 us -> none  [body(): lax.dot_general(local_rows.reshape(col_count, row_share, col_blocks * blo...]
    psum x2 -> x1, waiting for transfers between devices: 52.7 us -> 64 us  [body(): packed = lax.psum(jnp.concatenate([heads, info_rows], axis=0), 'row')]
    ppermute x0 -> x4, starting transfers between devices: none -> 10.7 us  [col_sum(): lax.ppermute(block, 'col', [(i, i ^ step) for i in range(count)])]
  transfers between devices with their start and end apart: 3 -> 6, of which waited for: 2 -> 5; matrix products, arithmetic and copies ran while one was open for 58% -> 22% of each run, Pallas kernels for 0% -> 0%
where the time goes in v2:
time: 229 us; the launch traced here: 226 us
  waiting for transfers between devices  96.4 us (42%)
  other arithmetic  55.9 us (24%)
  matrix products  41.3 us (18%)
  between operations  13.7 us (6%)
  starting transfers between devices  10.9 us (5%)
  local copies, waits for them, and re-layouts  7.55 us (3%)
    psum x1, waiting for transfers between devices, body(): packed = lax.psum(jnp.concatenate([heads, info_rows], axis=0), 'row')  64 us
    dot_general x7, matrix products, times_transposed(): lax.dot_general(left_mat, right_mat, (((1,), (1,)), ((), ())), precision=...  40.7 us
    ppermute x4, waiting for transfers between devices, col_sum(): lax.ppermute(block, 'col', [(i, i ^ step) for i in range(count)])  32.4 us
    another operation x6, other arithmetic, lower_inverse(): factor = jnp.linalg.cholesky(square)  24.8 us
    another operation x4, other arithmetic, lower_inverse(): jax.scipy.linalg.solve_triangular(factor, jnp.eye(square.shape[0], dtype=...  21.2 us
    ppermute x4, starting transfers between devices, col_sum(): lax.ppermute(block, 'col', [(i, i ^ step) for i in range(count)])  10.7 us
    select_n x1, other arithmetic, body(): jnp.where(is_first, head_rows, 0.0)  6.91 us
  transfers between devices with their start and end apart: 6, of which 5 were waited for; matrix products, arithmetic and copies ran while one was open for 22% of the time, Pallas kernels for 0%

profile of v2, /device:TPU:4, one launch (start us, length us, event | category | flops | bytes accessed | tf_op | source)
XLA Modules:
  0.0 225.8 jit_solution(17675555234033417536)
XLA Ops:
  6.5 0.7 and_select_fusion.1
  7.2 0.7 slice_bitcast_fusion.8
  7.9 6.9 %fusion.9 = (f32[128,16,128]{2,1,0:T(8,128)S(1)}, f32[128,16,128]{2,1,0:T(8,128)S(1)}) fusion(pred[]{:T(512)S(6)} %eq.34, f32[23,1,128,16,1,128]{5,4,3,2,1,0:T(1,128)} %param.12, pred[]{:T(512)S(6)} %eq.35), kind=kLoop, calls=%fused_computation.12 | loop fusion | flops 524288 | bytes 3145730 | tf_op jit(solution)/shard_map/jit(_where)/select_n | solution.py:82
  14.9 0.9 copy_bitcast_fusion
  15.7 1.5 pad_maximum_fusion
  17.5 64.0 %all-reduce.4.cloned.1.call-done = f32[264,2048]{1,0:T(8,128)} async-done(((f32[264,2048]{1,0:T(8,128)}), f32[264,2048]{1,0:T(8,128)}) %all-reduce.4.cloned.1.call-update) | async-done | bytes 2162704 | tf_op jit(solution)/shard_map/psum | solution.py:88
  81.5 37.0 %fusion.3 = f32[2944,256]{0,1:T(8,128)S(1)} fusion(f32[368,8,16,128]{3,2,1,0:T(8,128)} %bitcast.101, f32[264,2048]{1,0:T(8,128)} %all-reduce.4.cloned.1.call-done), kind=kOutput, calls=%fused_computation.3 | convolution fusion | flops 18522046464 | bytes 29229056 | tf_op jit(solution)/shard_map/dot_general | solution.py:34
  118.5 2.3 %copy.30 = f32[2944,256]{1,0:T(8,128)} copy(f32[2944,256]{0,1:T(8,128)S(1)} %fusion.3) | data formatting | bytes 6029312 | tf_op jit(solution)/shard_map/dot_general | solution.py:34
  120.8 1.6 copy-done
  122.4 1.9 fusion.6
  124.3 1.6 collective-permute-start
  125.8 7.6 %collective-permute-done = f32[256,256]{0,1:T(8,128)S(1)} collective-permute-done((f32[256,256]{0,1:T(8,128)S(1)}, f32[256,256]{0,1:T(8,128)S(1)}, u32[]{:S(2)}, u32[]{:S(2)}) %collective-permute-start) | collective-permute-done | bytes 262176 | tf_op jit(solution)/shard_map/ppermute | solution.py:54
  133.5 3.1 %collective-permute-start.1 = (f32[256,256]{0,1:T(8,128)S(1)}, f32[256,256]{0,1:T(8,128)S(1)}, u32[]{:S(2)}, u32[]{:S(2)}) collective-permute-start(f32[256,256]{0,1:T(8,128)S(1)} %add.162), channel_id=1, source_target_pairs={{0,2},{1,3},{2,0},{3,1},{4,6},{5,7},{6,4},{7,5},{8,10},{9,11},{10,... | collective-permute-start | bytes 786440 | tf_op jit(solution)/shard_map/ppermute | solution.py:54
  136.6 8.9 %collective-permute-done.1 = f32[256,256]{0,1:T(8,128)S(1)} collective-permute-done((f32[256,256]{0,1:T(8,128)S(1)}, f32[256,256]{0,1:T(8,128)S(1)}, u32[]{:S(2)}, u32[]{:S(2)}) %collective-permute-start.1) | collective-permute-done | bytes 262176 | tf_op jit(solution)/shard_map/ppermute | solution.py:54
  145.5 2.0 collective-permute-start.2
  147.6 8.1 %collective-permute-done.2 = f32[256,256]{0,1:T(8,128)S(1)} collective-permute-done((f32[256,256]{0,1:T(8,128)S(1)}, f32[256,256]{0,1:T(8,128)S(1)}, u32[]{:S(2)}, u32[]{:S(2)}) %collective-permute-start.2) | collective-permute-done | bytes 262176 | tf_op jit(solution)/shard_map/ppermute | solution.py:54
  155.7 4.1 %collective-permute-start.3 = (f32[256,256]{0,1:T(8,128)S(1)}, f32[256,256]{0,1:T(8,128)S(1)}, u32[]{:S(2)}, u32[]{:S(2)}) collective-permute-start(f32[256,256]{0,1:T(8,128)S(1)} %add.164), channel_id=1, source_target_pairs={{0,8},{1,9},{2,10},{3,11},{4,12},{5,13},{6,14},{7,15},{8,0},{9,1},... | collective-permute-start | bytes 786440 | tf_op jit(solution)/shard_map/ppermute | solution.py:54
  160.0 7.8 %collective-permute-done.3 = f32[256,256]{0,1:T(8,128)S(1)} collective-permute-done((f32[256,256]{0,1:T(8,128)S(1)}, f32[256,256]{0,1:T(8,128)S(1)}, u32[]{:S(2)}, u32[]{:S(2)}) %collective-permute-start.3) | collective-permute-done | bytes 262176 | tf_op jit(solution)/shard_map/ppermute | solution.py:54
  168.3 11.7 %cholesky.44 = f32[128,128]{1,0:T(8,128)S(1)} custom-call(f32[128,128]{1,0:T(8,128)S(1)} %fusion.28), custom_call_target="Cholesky" | custom-call | tf_op jit(solution)/shard_map/jit(cholesky)/cholesky | solution.py:44
  180.0 0.6 compare_reduce_fusion.1
  180.7 0.7 fusion.15
  181.3 9.8 %custom-call.6 = f32[1,128,128]{1,2,0:T(8,128)S(1)} custom-call(f32[1,128,128]{2,1,0:T(8,128)S(1)} %fusion.15), custom_call_target="InvertDiagBlocksLowerTriangular" | custom-call | tf_op jit(solution)/shard_map/jit(_solve_triangular)/triangular_solve | solution.py:45
  191.4 0.4 fusion.23
  192.2 11.7 %cholesky.55 = f32[128,128]{1,0:T(8,128)S(1)} custom-call(f32[128,128]{1,0:T(8,128)S(1)} %fusion.26), custom_call_target="Cholesky" | custom-call | tf_op jit(solution)/shard_map/jit(cholesky)/cholesky | solution.py:44
  204.0 0.6 compare_reduce_fusion
  204.6 0.7 fusion.16
  205.3 10.0 %custom-call.7 = f32[1,128,128]{1,2,0:T(8,128)S(1)} custom-call(f32[1,128,128]{2,1,0:T(8,128)S(1)} %fusion.16), custom_call_target="InvertDiagBlocksLowerTriangular" | custom-call | tf_op jit(solution)/shard_map/jit(_solve_triangular)/triangular_solve | solution.py:45
  215.6 1.1 copy.31
  216.9 0.4 fusion.65
  217.3 0.4 convolution_subtract_fusion
  217.7 0.4 convolution_bitcast_fusion
  218.2 0.8 copy.39
  (39 shorter events, 2.4 us)
Async XLA Ops:
  6.5 74.9 %all-reduce.4.cloned.1.call-start = ((), (), s32[]{:S(2)}) async-start(), calls=%async_computation.1 | async-start | bytes 4325376 | tf_op jit(solution)/shard_map/psum | solution.py:88
  17.3 198.4 %reduce-scatter.4.cloned.1.call-start = ((), (), s32[]{:S(2)}) async-start(), calls=%async_computation.2 | async-start | bytes 3203072
  120.8 1.6 copy-start
  122.4 25.1 %copy-start.1 = (s32[23,1,128]{2,1,0:T(1,128)S(1)}, s32[23,1,128]{2,1,0:T(1,128)}, u32[]{:S(2)}) copy-start(s32[23,1,128]{2,1,0:T(1,128)} %param.13) | copy-start | bytes 35332
  122.4 37.4 %copy-start.2 = (f32[23,1,128]{2,1,0:T(1,128)S(1)}, f32[23,1,128]{2,1,0:T(1,128)}, u32[]{:S(2)}) copy-start(f32[23,1,128]{2,1,0:T(1,128)} %param.14) | copy-start | bytes 35332
  124.3 9.2 %collective-permute-start = (f32[256,256]{0,1:T(8,128)S(1)}, f32[256,256]{0,1:T(8,128)S(1)}, u32[]{:S(2)}, u32[]{:S(2)}) collective-permute-start(f32[256,256]{0,1:T(8,128)S(1)} %fusion.6), channel_id=1, source_target_pairs={{0,1},{1,0},{2,3},{3,2},{4,5},{5,4},{6,7},{7,6},{8,9},{9,8},{10,11... | collective-permute-start | bytes 786440 | tf_op jit(solution)/shard_map/ppermute | solution.py:54
  133.5 12.0 %collective-permute-start.1 = (f32[256,256]{0,1:T(8,128)S(1)}, f32[256,256]{0,1:T(8,128)S(1)}, u32[]{:S(2)}, u32[]{:S(2)}) collective-permute-start(f32[256,256]{0,1:T(8,128)S(1)} %add.162), channel_id=1, source_target_pairs={{0,2},{1,3},{2,0},{3,1},{4,6},{5,7},{6,4},{7,5},{8,10},{9,11},{10,... | collective-permute-start | bytes 786440 | tf_op jit(solution)/shard_map/ppermute | solution.py:54
  145.5 10.2 %collective-permute-start.2 = (f32[256,256]{0,1:T(8,128)S(1)}, f32[256,256]{0,1:T(8,128)S(1)}, u32[]{:S(2)}, u32[]{:S(2)}) collective-permute-start(f32[256,256]{0,1:T(8,128)S(1)} %add.163), channel_id=1, source_target_pairs={{0,4},{1,5},{2,6},{3,7},{4,0},{5,1},{6,2},{7,3},{8,12},{9,13},{10,... | collective-permute-start | bytes 786440 | tf_op jit(solution)/shard_map/ppermute | solution.py:54
  155.7 12.1 %collective-permute-start.3 = (f32[256,256]{0,1:T(8,128)S(1)}, f32[256,256]{0,1:T(8,128)S(1)}, u32[]{:S(2)}, u32[]{:S(2)}) collective-permute-start(f32[256,256]{0,1:T(8,128)S(1)} %add.164), channel_id=1, source_target_pairs={{0,8},{1,9},{2,10},{3,11},{4,12},{5,13},{6,14},{7,15},{8,0},{9,1},... | collective-permute-start | bytes 786440 | tf_op jit(solution)/shard_map/ppermute | solution.py:54
Sparse Core Ops, SparseCore 0:
  17.4 64.0 all-reduce.3
  120.9 83.4 reduce-scatter.3

commit v3 on v2

--- a/solution.py
+++ b/solution.py
@@ -56,6 +56,39 @@
     return block
 
 
+def row_broadcast(pack):
+    row = lax.axis_index("row")
+    swap01 = lax.ppermute(pack, "row", [(0, 1), (1, 0)])
+    to_next = lax.ppermute(pack, "row", [(0, 2), (1, 3)])
+    to_prev = lax.ppermute(pack, "row", [(0, 6), (1, 7)])
+    hand = jnp.where(row < 4, to_next, to_prev)
+    swap_side = lax.ppermute(hand, "row", [(2, 3), (3, 2), (6, 7), (7, 6)])
+    to_far = lax.ppermute(to_next, "row", [(2, 4), (3, 5)])
+    swap_far = lax.ppermute(to_far, "row", [(4, 5), (5, 4)])
+    chip = row // 2
+    first_hand = jnp.where(
+        chip == 0, pack, jnp.where(chip == 1, to_next, jnp.where(chip == 2, to_far, to_prev))
+    )
+    second_hand = jnp.where(chip == 0, swap01, jnp.where(chip == 2, swap_far, swap_side))
+    return first_hand, second_hand
+
+
+def col_scatter(blocks):
+    count = lax.axis_size("col")
+    me = lax.axis_index("col")
+    bits = count.bit_length() - 1
+    shaped = blocks.reshape((2,) * bits + blocks.shape[1:])
+    remaining = list(range(bits - 1, -1, -1))
+    for bit in (0, 2, 1, 3)[:bits] if bits == 4 else range(bits):
+        axis = remaining.index(bit)
+        mine = (me >> bit) % 2
+        keep = lax.dynamic_index_in_dim(shaped, mine, axis, keepdims=False)
+        send = lax.dynamic_index_in_dim(shaped, 1 - mine, axis, keepdims=False)
+        shaped = keep + lax.ppermute(send, "col", [(i, i ^ (1 << bit)) for i in range(count)])
+        remaining.pop(axis)
+    return shaped
+
+
 def body(left_factor, pick_site, noise):
     row_blocks, _, block_width, col_blocks, _, _ = left_factor.shape
     col_count = lax.axis_size("col")
@@ -78,20 +111,21 @@
     )
     is_first = row_index == 0
     is_second = row_index == 1
-    heads = jnp.concatenate(
-        [jnp.where(is_first, head_rows, 0.0), jnp.where(is_second, head_rows, 0.0)], axis=0
+    info_rows = jnp.zeros((8, head_rows.shape[1]), jnp.float32).at[:4, :block_width].set(head_info)
+    first_hand, second_hand = row_broadcast(jnp.concatenate([head_rows, info_rows], axis=0))
+    is_even = row_index % 2 == 0
+    first_pack = jnp.where(is_even, first_hand, second_hand)
+    second_pack = jnp.where(is_even, second_hand, first_hand)
+    heads = jnp.concatenate([first_pack[:block_width], second_pack[:block_width]], axis=0)
+    info = jnp.concatenate(
+        [first_pack[block_width : block_width + 4, :block_width],
+         second_pack[block_width : block_width + 4, :block_width]],
+        axis=1,
     )
-    info = jnp.concatenate(
-        [jnp.where(is_first, head_info, 0.0), jnp.where(is_second, head_info, 0.0)], axis=1
-    )
-    info_rows = jnp.zeros((8, heads.shape[1]), jnp.float32).at[:4, : 2 * block_width].set(info)
-    packed = lax.psum(jnp.concatenate([heads, info_rows], axis=0), "row")
-    heads = packed[: 2 * block_width]
-    info = packed[2 * block_width : 2 * block_width + 4, : 2 * block_width]
 
+    gram = col_sum(times_transposed(heads, heads))
     terms = times_transposed(local_rows, heads).reshape(col_count, row_share, 2 * block_width)
-    sums = lax.psum_scatter(terms, "col", scatter_dimension=0, tiled=False)
-    gram = col_sum(times_transposed(heads, heads))
+    sums = col_scatter(terms)
 
     first_coords = info[:3, :block_width]
     second_coords = info[:3, block_width:]

time: 229 us -> 209 us (0.913); the launches traced: 226 us -> 209 us
  waiting for transfers between devices: 96.4 us -> 67.6 us
  starting transfers between devices: 10.9 us -> 24.3 us
  between operations: 13.7 us -> 0.54 us
  local copies, waits for them, and re-layouts: 7.55 us -> 16.2 us
  other arithmetic: 55.9 us -> 59.1 us
    psum x1 -> x0, waiting for transfers between devices: 64 us -> none  [body(): packed = lax.psum(jnp.concatenate([heads, info_rows], axis=0), 'row')]
    ppermute x0 -> x10, waiting for transfers between devices: none -> 57.5 us  [the longest x1 46.7 us: row_broadcast(): to_far = lax.ppermute(to_next, 'row', [(2, 4), (3, 5)])]
    ppermute x4, waiting for transfers between devices: 32.4 us -> 10 us  [col_sum(): lax.ppermute(block, 'col', [(i, i ^ step) for i in range(count)])]
    ppermute x0 -> x10, starting transfers between devices: none -> 13.2 us  [the longest x4 5.12 us: col_scatter(): lax.ppermute(send, 'col', [(i, i ^ 1 << bit) for i in range(count)])]
    slice x0 -> x3, local copies, waits for them, and re-layouts: none -> 4.12 us  [the longest x1 3.97 us: body(): head_rows = local_rows[:block_width]]
    select_n x2 -> x3, other arithmetic: 6.92 us -> 3.59 us  [the longest x1 2.34 us: body(): first_pack = jnp.where(is_even, first_hand, second_hand)]
    add x0 -> x4, other arithmetic: none -> 2.91 us  [col_scatter(): keep + lax.ppermute(send, 'col', [(i, i ^ 1 << bit) for i in range(count)])]
    squeeze x0 -> x3, local copies, waits for them, and re-layouts: none -> 2.87 us  [col_scatter(): send = lax.dynamic_index_in_dim(shaped, 1 - mine, axis, keepdims=False)]
  transfers between devices with their start and end apart: 6 -> 14, of which waited for: 5 -> 8; matrix products, arithmetic and copies ran while one was open for 22% -> 46% of each run, Pallas kernels for 0% -> 0%
where the time goes in v3:
time: 209 us
  waiting for transfers between devices  67.6 us (32%)
  other arithmetic  59.1 us (28%)
  matrix products  41.2 us (20%)
  starting transfers between devices  24.3 us (12%)
  local copies, waits for them, and re-layouts  16.2 us (8%)
    ppermute x1, waiting for transfers between devices, row_broadcast(): to_far = lax.ppermute(to_next, 'row', [(2, 4), (3, 5)])  46.7 us
    dot_general x7, matrix products, times_transposed(): lax.dot_general(left_mat, right_mat, (((1,), (1,)), ((), ())), precision=...  40.7 us
    another operation x6, other arithmetic, lower_inverse(): factor = jnp.linalg.cholesky(square)  24.9 us
    another operation x4, other arithmetic, lower_inverse(): jax.scipy.linalg.solve_triangular(factor, jnp.eye(square.shape[0], dtype=...  20.9 us
    ppermute x4, starting transfers between devices, col_sum(): lax.ppermute(block, 'col', [(i, i ^ step) for i in range(count)])  11.1 us
    ppermute x4, waiting for transfers between devices, col_sum(): lax.ppermute(block, 'col', [(i, i ^ step) for i in range(count)])  10 us
    ppermute x4, waiting for transfers between devices, col_scatter(): lax.ppermute(send, 'col', [(i, i ^ 1 << bit) for i in range(count)])  7.8 us
    ppermute x4, starting transfers between devices, col_scatter(): lax.ppermute(send, 'col', [(i, i ^ 1 << bit) for i in range(count)])  5.12 us
  transfers between devices with their start and end apart: 14, of which 8 were waited for; matrix products, arithmetic and copies ran while one was open for 46% of the time, Pallas kernels for 0%

profile of v3, /device:TPU:4, one launch (start us, length us, event | category | flops | bytes accessed | tf_op | source)
XLA Modules:
  0.0 208.9 jit_solution(4071273510263245861)
XLA Ops:
  1.3 4.0 %slice_reduce_fusion = f32[128,16,128]{2,1,0:T(8,128)S(1)} fusion(f32[23,1,128,16,1,128]{5,4,3,2,1,0:T(1,128)} %param.12), kind=kLoop, calls=%fused_computation.13 | loop fusion | bytes 2097152 | tf_op jit(solution)/shard_map/slice | solution.py:108
  8.3 1.3 collective-permute-start.1
  9.6 1.7 collective-permute-start.3
  11.2 1.1 broadcast_select_fusion
  12.4 1.7 collective-permute-start.5
  14.1 46.7 %collective-permute-done.1 = f32[136,2048]{1,0:T(8,128)} collective-permute-done((f32[136,2048]{1,0:T(8,128)S(1)}, f32[136,2048]{1,0:T(8,128)}, u32[]{:S(2)}, u32[]{:S(2)}) %collective-permute-start.1) | collective-permute-done | bytes 1114144 | tf_op jit(solution)/shard_map/ppermute | solution.py:66
  60.8 1.9 collective-permute-start.4
  62.8 3.0 %collective-permute-done.4 = f32[136,2048]{1,0:T(8,128)} collective-permute-done((f32[136,2048]{1,0:T(8,128)}, f32[136,2048]{1,0:T(8,128)}, u32[]{:S(2)}, u32[]{:S(2)}) %collective-permute-start.4) | collective-permute-done | bytes 1114144 | tf_op jit(solution)/shard_map/ppermute | solution.py:67
  65.8 2.3 %broadcast_select_fusion.2 = (f32[136,2048]{1,0:T(8,128)S(1)}, f32[136,2048]{1,0:T(8,128)S(1)}, f32[136,2048]{1,0:T(8,128)S(1)}) fusion(pred[]{:T(512)S(6)} %eq.52, f32[136,2048]{1,0:T(8,128)S(1)} %collective-permute-done, f32[136,2048]{1,0:T(8,128)} %collective-permute-done.1, f32[136,2048]{1,0:T(8,128)S(1)} %collective-permute-done.2, pred[]{:T(512)S(6)} %eq.55, ...), kind=kLoop, calls=%fused_computation.18 | loop fusion | flops 1949696 | bytes 11141124 | tf_op jit(solution)/shard_map/jit(_where)/select_n | solution.py:117
  69.6 1.9 fusion.6
  71.5 1.7 collective-permute-start.10
  73.1 6.8 %collective-permute-done.10 = f32[256,256]{0,1:T(8,128)S(1)} collective-permute-done((f32[256,256]{0,1:T(8,128)S(1)}, f32[256,256]{0,1:T(8,128)S(1)}, u32[]{:S(2)}, u32[]{:S(2)}) %collective-permute-start.10) | collective-permute-done | bytes 262176 | tf_op jit(solution)/shard_map/ppermute | solution.py:54
  80.0 3.5 %collective-permute-start.11 = (f32[256,256]{0,1:T(8,128)S(1)}, f32[256,256]{0,1:T(8,128)}, u32[]{:S(2)}, u32[]{:S(2)}) collective-permute-start(f32[256,256]{0,1:T(8,128)S(1)} %add.236), channel_id=1, source_target_pairs={{0,2},{1,3},{2,0},{3,1},{4,6},{5,7},{6,4},{7,5},{8,10},{9,11},{10,... | collective-permute-start | bytes 786440 | tf_op jit(solution)/shard_map/ppermute | solution.py:54
  83.4 37.0 %fusion.3 = f32[2944,256]{0,1:T(8,128)S(1)} fusion(f32[368,8,16,128]{3,2,1,0:T(8,128)} %bitcast.112, f32[128,2048]{1,0:T(8,128)} %copy-done.4, f32[128,2048]{1,0:T(8,128)} %copy-done.5), kind=kOutput, calls=%fused_computation.3 | convolution fusion | flops 18522570752 | bytes 29229056 | tf_op jit(solution)/shard_map/dot_general | solution.py:34
  120.4 2.3 %copy.24 = f32[2944,256]{1,0:T(8,128)} copy(f32[2944,256]{0,1:T(8,128)S(1)} %fusion.3) | data formatting | bytes 6029312 | tf_op jit(solution)/shard_map/dot_general | solution.py:34
  123.7 2.0 collective-permute-start.12
  125.7 2.8 %dynamic-slice_bitcast_fusion = f32[2,2,2,184,256]{4,3,2,1,0:T(8,128)} fusion(f32[2,2,2,2,184,256]{5,4,3,2,1,0:T(8,128)} %bitcast.113, s32[]{:T(128)S(6)} %select_n.221), kind=kLoop, calls=%fused_computation.7 | loop fusion | bytes 3014660 | tf_op jit(solution)/shard_map/jit(dynamic_index_in_dim)/squeeze | solution.py:86
  129.3 2.0 collective-permute-done.12
  132.3 4.0 %collective-permute-start.13 = (f32[256,256]{0,1:T(8,128)S(1)}, f32[256,256]{0,1:T(8,128)}, u32[]{:S(2)}, u32[]{:S(2)}) collective-permute-start(f32[256,256]{0,1:T(8,128)S(1)} %add.238), channel_id=1, source_target_pairs={{0,8},{1,9},{2,10},{3,11},{4,12},{5,13},{6,14},{7,15},{8,0},{9,1},... | collective-permute-start | bytes 786440 | tf_op jit(solution)/shard_map/ppermute | solution.py:54
  138.2 1.5 slice_bitcast_fusion
  139.7 1.3 collective-permute-done.13
  142.4 11.7 %cholesky.44 = f32[128,128]{1,0:T(8,128)S(1)} custom-call(f32[128,128]{1,0:T(8,128)S(1)} %fusion.25), custom_call_target="Cholesky" | custom-call | tf_op jit(solution)/shard_map/jit(cholesky)/cholesky | solution.py:44
  155.5 9.8 %custom-call.6 = f32[1,128,128]{1,2,0:T(8,128)S(1)} custom-call(f32[1,128,128]{2,1,0:T(8,128)S(1)} %fusion.12), custom_call_target="InvertDiagBlocksLowerTriangular" | custom-call | tf_op jit(solution)/shard_map/jit(_solve_triangular)/triangular_solve | solution.py:45
  165.3 1.6 bitcast_add_fusion
  166.9 1.1 copy-done.1
  168.1 1.4 collective-permute-start.7
  170.6 11.7 %cholesky.55 = f32[128,128]{1,0:T(8,128)S(1)} custom-call(f32[128,128]{1,0:T(8,128)S(1)} %fusion.23), custom_call_target="Cholesky" | custom-call | tf_op jit(solution)/shard_map/jit(cholesky)/cholesky | solution.py:44
  182.3 2.2 %collective-permute-done.7 = f32[2,2,184,256]{3,2,1,0:T(8,128)S(1)} collective-permute-done((f32[2,2,184,256]{3,2,1,0:T(8,128)S(1)}, f32[2,2,184,256]{3,2,1,0:T(8,128)S(1)}, u32[]{:S(2)}, u32[]{:S(2)}) %collective-permute-start.7) | collective-permute-done | bytes 753696 | tf_op jit(solution)/shard_map/ppermute | solution.py:87
  184.5 1.2 bitcast_add_fusion.1
  188.0 9.8 %custom-call.7 = f32[1,128,128]{1,2,0:T(8,128)S(1)} custom-call(f32[1,128,128]{2,1,0:T(8,128)S(1)} %fusion.13), custom_call_target="InvertDiagBlocksLowerTriangular" | custom-call | tf_op jit(solution)/shard_map/jit(_solve_triangular)/triangular_solve | solution.py:45
  198.6 2.4 %collective-permute-start.9 = (f32[184,256]{0,1:T(8,128)S(1)}, f32[184,256]{0,1:T(8,128)S(1)}, u32[]{:S(2)}, u32[]{:S(2)}) collective-permute-start(f32[184,256]{0,1:T(8,128)S(1)} %dynamic-slice_bitcast_fusion.2), channel_id=1, source_target_pairs={{0,8},{1,9},{2,10},{3,11},{4,12},{5,13},{6,14},{7,15},{8,0},{9,1},... | collective-permute-start | bytes 565256 | tf_op jit(solution)/shard_map/ppermute | solution.py:87
  201.3 5.2 %collective-permute-done.9 = f32[184,256]{0,1:T(8,128)S(1)} collective-permute-done((f32[184,256]{0,1:T(8,128)S(1)}, f32[184,256]{0,1:T(8,128)S(1)}, u32[]{:S(2)}, u32[]{:S(2)}) %collective-permute-start.9) | collective-permute-done | bytes 188448 | tf_op jit(solution)/shard_map/ppermute | solution.py:87
  (90 shorter events, 19.8 us)
Async XLA Ops:
  6.8 1.5 collective-permute-start
  7.5 3.7 %collective-permute-start.2 = (f32[136,2048]{1,0:T(8,128)}, f32[136,2048]{1,0:T(8,128)S(1)}, u32[]{:S(2)}, u32[]{:S(2)}) collective-permute-start(f32[136,2048]{1,0:T(8,128)} %pad_maximum_fusion.3), channel_id=1, source_target_pairs={{0,96},{16,112},{1,97},{17,113},{2,98},{18,114},{3,99},{19,115},{4... | collective-permute-start | bytes 3342344 | tf_op jit(solution)/shard_map/ppermute | solution.py:63
  8.3 52.5 %collective-permute-start.1 = (f32[136,2048]{1,0:T(8,128)S(1)}, f32[136,2048]{1,0:T(8,128)}, u32[]{:S(2)}, u32[]{:S(2)}) collective-permute-start(f32[136,2048]{1,0:T(8,128)S(1)} %collective-permute-done), channel_id=1, source_target_pairs={{32,64},{48,80},{33,65},{49,81},{34,66},{50,82},{35,67},{51,83},{3... | collective-permute-start | bytes 3342344 | tf_op jit(solution)/shard_map/ppermute | solution.py:66
  9.6 53.2 %collective-permute-start.3 = (f32[136,2048]{1,0:T(8,128)}, f32[136,2048]{1,0:T(8,128)}, u32[]{:S(2)}, u32[]{:S(2)}) collective-permute-start(f32[136,2048]{1,0:T(8,128)} %pad_maximum_fusion.3), channel_id=1, source_target_pairs={{0,16},{16,0},{1,17},{17,1},{2,18},{18,2},{3,19},{19,3},{4,20},{20... | collective-permute-start | bytes 3342344 | tf_op jit(solution)/shard_map/ppermute | solution.py:61
  12.4 50.4 %collective-permute-start.5 = (f32[136,2048]{1,0:T(8,128)}, f32[136,2048]{1,0:T(8,128)}, u32[]{:S(2)}, u32[]{:S(2)}) collective-permute-start(f32[136,2048]{1,0:T(8,128)} %broadcast_select_fusion), channel_id=1, source_target_pairs={{32,48},{48,32},{96,112},{112,96},{33,49},{49,33},{97,113},{113,97... | collective-permute-start | bytes 3342344 | tf_op jit(solution)/shard_map/ppermute | solution.py:65
  60.8 5.0 %collective-permute-start.4 = (f32[136,2048]{1,0:T(8,128)}, f32[136,2048]{1,0:T(8,128)}, u32[]{:S(2)}, u32[]{:S(2)}) collective-permute-start(f32[136,2048]{1,0:T(8,128)} %collective-permute-done.1), channel_id=1, source_target_pairs={{64,80},{80,64},{65,81},{81,65},{66,82},{82,66},{67,83},{83,67},{6... | collective-permute-start | bytes 3342344 | tf_op jit(solution)/shard_map/ppermute | solution.py:67
  68.1 1.4 copy-start.2
  68.3 1.1 copy-start.3
  69.5 2.0 copy-start.4
  69.6 1.9 copy-start.5
  71.5 8.4 %collective-permute-start.10 = (f32[256,256]{0,1:T(8,128)S(1)}, f32[256,256]{0,1:T(8,128)S(1)}, u32[]{:S(2)}, u32[]{:S(2)}) collective-permute-start(f32[256,256]{0,1:T(8,128)S(1)} %fusion.6), channel_id=1, source_target_pairs={{0,1},{1,0},{2,3},{3,2},{4,5},{5,4},{6,7},{7,6},{8,9},{9,8},{10,11... | collective-permute-start | bytes 786440 | tf_op jit(solution)/shard_map/ppermute | solution.py:54
  80.0 42.7 %collective-permute-start.11 = (f32[256,256]{0,1:T(8,128)S(1)}, f32[256,256]{0,1:T(8,128)}, u32[]{:S(2)}, u32[]{:S(2)}) collective-permute-start(f32[256,256]{0,1:T(8,128)S(1)} %add.236), channel_id=1, source_target_pairs={{0,2},{1,3},{2,0},{3,1},{4,6},{5,7},{6,4},{7,5},{8,10},{9,11},{10,... | collective-permute-start | bytes 786440 | tf_op jit(solution)/shard_map/ppermute | solution.py:54
  122.7 6.5 %copy-start.6 = (s32[23,1,128]{2,1,0:T(1,128)S(1)}, s32[23,1,128]{2,1,0:T(1,128)}, u32[]{:S(2)}) copy-start(s32[23,1,128]{2,1,0:T(1,128)} %param.13) | copy-start | bytes 35332
  123.7 7.6 %collective-permute-start.12 = (f32[256,256]{0,1:T(8,128)S(1)}, f32[256,256]{0,1:T(8,128)}, u32[]{:S(2)}, u32[]{:S(2)}) collective-permute-start(f32[256,256]{0,1:T(8,128)S(1)} %add.237), channel_id=1, source_target_pairs={{0,4},{1,5},{2,6},{3,7},{4,0},{5,1},{6,2},{7,3},{8,12},{9,13},{10,... | collective-permute-start | bytes 786440 | tf_op jit(solution)/shard_map/ppermute | solution.py:54
  125.7 39.6 %copy-start = (f32[2944,256]{1,0:T(8,128)S(1)}, f32[2944,256]{1,0:T(8,128)}, u32[]{:S(2)}) copy-start(f32[2944,256]{1,0:T(8,128)} %copy.24) | copy-start | bytes 9043972
  128.5 36.8 %collective-permute-start.6 = (f32[2,2,2,184,256]{4,3,2,1,0:T(8,128)}, f32[2,2,2,184,256]{4,3,2,1,0:T(8,128)}, u32[]{:S(2)}, u32[]{:S(2)}) collective-permute-start(f32[2,2,2,184,256]{4,3,2,1,0:T(8,128)} %dynamic-slice_bitcast_fusion), channel_id=1, source_target_pairs={{0,1},{1,0},{2,3},{3,2},{4,5},{5,4},{6,7},{7,6},{8,9},{9,8},{10,11... | collective-permute-start | bytes 4521992 | tf_op jit(solution)/shard_map/ppermute | solution.py:87
  132.3 8.7 %collective-permute-start.13 = (f32[256,256]{0,1:T(8,128)S(1)}, f32[256,256]{0,1:T(8,128)}, u32[]{:S(2)}, u32[]{:S(2)}) collective-permute-start(f32[256,256]{0,1:T(8,128)S(1)} %add.238), channel_id=1, source_target_pairs={{0,8},{1,9},{2,10},{3,11},{4,12},{5,13},{6,14},{7,15},{8,0},{9,1},... | collective-permute-start | bytes 786440 | tf_op jit(solution)/shard_map/ppermute | solution.py:54
  166.9 1.1 copy-start.1
  168.0 1.7 copy-start.11
  168.0 1.8 copy-start.12
  168.1 1.8 copy-start.13
  168.1 2.2 %copy-start.14 = (f32[128]{0:T(128)S(1)}, f32[128]{0:T(128)}, u32[]{:S(2)}) copy-start(f32[128]{0:T(128)} %get-tuple-element.48) | copy-start | bytes 1540
  168.1 16.4 %collective-permute-start.7 = (f32[2,2,184,256]{3,2,1,0:T(8,128)S(1)}, f32[2,2,184,256]{3,2,1,0:T(8,128)S(1)}, u32[]{:S(2)}, u32[]{:S(2)}) collective-permute-start(f32[2,2,184,256]{3,2,1,0:T(8,128)S(1)} %dynamic-slice_bitcast_fusion.1), channel_id=1, source_target_pairs={{0,4},{1,5},{2,6},{3,7},{4,0},{5,1},{6,2},{7,3},{8,12},{9,13},{10,... | collective-permute-start | bytes 2261000 | tf_op jit(solution)/shard_map/ppermute | solution.py:87
  186.0 12.4 %collective-permute-start.8 = (f32[2,184,256]{1,2,0:T(8,128)S(1)}, f32[2,184,256]{1,2,0:T(8,128)S(1)}, u32[]{:S(2)}, u32[]{:S(2)}) collective-permute-start(f32[2,184,256]{1,2,0:T(8,128)S(1)} %bitcast.118), channel_id=1, source_target_pairs={{0,2},{1,3},{2,0},{3,1},{4,6},{5,7},{6,4},{7,5},{8,10},{9,11},{10,... | collective-permute-start | bytes 1130504 | tf_op jit(solution)/shard_map/ppermute | solution.py:87
  198.5 8.1 %copy-start.7 = (f32[1,184]{1,0:T(1,128)S(1)}, f32[1,184]{1,0:T(1,128)}, u32[]{:S(2)}) copy-start(f32[1,184]{1,0:T(1,128)} %get-tuple-element.62) | copy-start | bytes 2212
  198.5 8.1 %copy-start.8 = (f32[1,184]{1,0:T(1,128)S(1)}, f32[1,184]{1,0:T(1,128)}, u32[]{:S(2)}) copy-start(f32[1,184]{1,0:T(1,128)} %get-tuple-element.63) | copy-start | bytes 2212
  198.5 8.1 %copy-start.9 = (f32[1,184]{1,0:T(1,128)S(1)}, f32[1,184]{1,0:T(1,128)}, u32[]{:S(2)}) copy-start(f32[1,184]{1,0:T(1,128)} %get-tuple-element.64) | copy-start | bytes 2212
  198.5 8.3 %copy-start.10 = (f32[128]{0:T(128)S(1)}, f32[128]{0:T(128)}, u32[]{:S(2)}) copy-start(f32[128]{0:T(128)} %slice.189) | copy-start | bytes 1540
  198.6 8.0 %collective-permute-start.9 = (f32[184,256]{0,1:T(8,128)S(1)}, f32[184,256]{0,1:T(8,128)S(1)}, u32[]{:S(2)}, u32[]{:S(2)}) collective-permute-start(f32[184,256]{0,1:T(8,128)S(1)} %dynamic-slice_bitcast_fusion.2), channel_id=1, source_target_pairs={{0,8},{1,9},{2,10},{3,11},{4,12},{5,13},{6,14},{7,15},{8,0},{9,1},... | collective-permute-start | bytes 565256 | tf_op jit(solution)/shard_map/ppermute | solution.py:87

commit v4 on v3

--- a/solution.py
+++ b/solution.py
@@ -49,28 +49,35 @@
 
 def col_sum(block):
     count = lax.axis_size("col")
-    step = 1
-    while step < count:
-        block = block + lax.ppermute(block, "col", [(i, i ^ step) for i in range(count)])
-        step *= 2
+    group = 1
+    while group < count:
+        width = min(4, count // group)
+        parts = [
+            lax.ppermute(block, "col", [(i, i ^ (k * group)) for i in range(count)])
+            for k in range(1, width)
+        ]
+        for part in parts:
+            block = block + part
+        group *= width
     return block
 
 
 def row_broadcast(pack):
     row = lax.axis_index("row")
-    swap01 = lax.ppermute(pack, "row", [(0, 1), (1, 0)])
-    to_next = lax.ppermute(pack, "row", [(0, 2), (1, 3)])
-    to_prev = lax.ppermute(pack, "row", [(0, 6), (1, 7)])
-    hand = jnp.where(row < 4, to_next, to_prev)
-    swap_side = lax.ppermute(hand, "row", [(2, 3), (3, 2), (6, 7), (7, 6)])
-    to_far = lax.ppermute(to_next, "row", [(2, 4), (3, 5)])
-    swap_far = lax.ppermute(to_far, "row", [(4, 5), (5, 4)])
-    chip = row // 2
-    first_hand = jnp.where(
-        chip == 0, pack, jnp.where(chip == 1, to_next, jnp.where(chip == 2, to_far, to_prev))
+    swap_home = lax.ppermute(pack, "row", [(0, 1), (1, 0)])
+    first_out = lax.ppermute(pack, "row", [(0, 2), (1, 7)])
+    relay = lax.ppermute(first_out, "row", [(2, 4), (7, 5)])
+    second_out = lax.ppermute(
+        jnp.where(row < 2, pack, first_out), "row", [(1, 3), (0, 6)]
     )
-    second_hand = jnp.where(chip == 0, swap01, jnp.where(chip == 2, swap_far, swap_side))
-    return first_hand, second_hand
+    hand = jnp.where(
+        row < 2,
+        pack,
+        jnp.where((row == 2) | (row == 7), first_out, jnp.where((row == 4) | (row == 5), relay, second_out)),
+    )
+    swap_far = lax.ppermute(hand, "row", [(2, 3), (3, 2), (4, 5), (5, 4), (6, 7), (7, 6)])
+    other = jnp.where(row < 2, swap_home, swap_far)
+    return hand, other
 
 
 def col_scatter(blocks):
@@ -112,10 +119,10 @@
     is_first = row_index == 0
     is_second = row_index == 1
     info_rows = jnp.zeros((8, head_rows.shape[1]), jnp.float32).at[:4, :block_width].set(head_info)
-    first_hand, second_hand = row_broadcast(jnp.concatenate([head_rows, info_rows], axis=0))
+    hand, other = row_broadcast(jnp.concatenate([head_rows, info_rows], axis=0))
     is_even = row_index % 2 == 0
-    first_pack = jnp.where(is_even, first_hand, second_hand)
-    second_pack = jnp.where(is_even, second_hand, first_hand)
+    first_pack = jnp.where(is_even, hand, other)
+    second_pack = jnp.where(is_even, other, hand)
     heads = jnp.concatenate([first_pack[:block_width], second_pack[:block_width]], axis=0)
     info = jnp.concatenate(
         [first_pack[block_width : block_width + 4, :block_width],

time: 209 us -> 190 us (0.909)
  waiting for transfers between devices: 67.6 us -> 51.3 us
  starting transfers between devices: 24.3 us -> 21.6 us
  other arithmetic: 59.1 us -> 56.7 us
    ppermute x10 -> x11, waiting for transfers between devices: 59.8 us -> 40.6 us  [the longest x1 27.8 us: row_broadcast(): relay = lax.ppermute(first_out, 'row', [(2, 4), (7, 5)])]
    ppermute x4, waiting for transfers between devices: 7.8 us -> 10.8 us  [col_scatter(): lax.ppermute(send, 'col', [(i, i ^ 1 << bit) for i in range(count)])]
    ppermute x10 -> x11, starting transfers between devices: 19.1 us -> 16.2 us  [the longest x6 9.91 us: col_sum(): lax.ppermute(block, 'col', [(i, i ^ k * group) for i in range(count)])]
    unnamed x31 -> x35, local copies, waits for them, and re-layouts: 2.68 us -> 4.8 us
  transfers between devices with their start and end apart: 14 -> 15, of which waited for: 8 -> 7; matrix products, arithmetic and copies ran while one was open for 46% -> 51% of each run, Pallas kernels for 0% -> 0%
where the time goes in v4:
time: 190 us; the launch traced here: 189 us
  other arithmetic  56.7 us (30%)
  waiting for transfers between devices  51.3 us (27%)
  matrix products  41 us (22%)
  starting transfers between devices  21.6 us (11%)
  local copies, waits for them, and re-layouts  18.1 us (10%)
    dot_general x7, matrix products, times_transposed(): lax.dot_general(left_mat, right_mat, (((1,), (1,)), ((), ())), precision=...  40.4 us
    ppermute x1, waiting for transfers between devices, row_broadcast(): relay = lax.ppermute(first_out, 'row', [(2, 4), (7, 5)])  27.8 us
    another operation x6, other arithmetic, lower_inverse(): factor = jnp.linalg.cholesky(square)  24.8 us
    another operation x4, other arithmetic, lower_inverse(): jax.scipy.linalg.solve_triangular(factor, jnp.eye(square.shape[0], dtype=...  20.8 us
    ppermute x4, waiting for transfers between devices, col_scatter(): lax.ppermute(send, 'col', [(i, i ^ 1 << bit) for i in range(count)])  10.8 us
    ppermute x6, waiting for transfers between devices, col_sum(): lax.ppermute(block, 'col', [(i, i ^ k * group) for i in range(count)])  10.2 us
    ppermute x6, starting transfers between devices, col_sum(): lax.ppermute(block, 'col', [(i, i ^ k * group) for i in range(count)])  9.91 us
    ppermute x4, starting transfers between devices, col_scatter(): lax.ppermute(send, 'col', [(i, i ^ 1 << bit) for i in range(count)])  5.4 us
  transfers between devices with their start and end apart: 15, of which 7 were waited for; matrix products, arithmetic and copies ran while one was open for 51% of the time, Pallas kernels for 0%

profile of v4, /device:TPU:4, one launch (start us, length us, event | category | flops | bytes accessed | tf_op | source)
XLA Modules:
  0.0 189.4 jit_solution(4951457999558863200)
XLA Ops:
  1.3 4.0 %slice_reduce_fusion = f32[128,16,128]{2,1,0:T(8,128)S(1)} fusion(f32[23,1,128,16,1,128]{5,4,3,2,1,0:T(1,128)} %param.12), kind=kLoop, calls=%fused_computation.12 | loop fusion | bytes 2097152 | tf_op jit(solution)/shard_map/slice | solution.py:115
  6.8 1.1 broadcast_select_fusion.1
  8.6 1.3 collective-permute-start.1
  9.9 1.7 collective-permute-start.3
  12.6 27.8 %collective-permute-done.1 = f32[136,2048]{1,0:T(8,128)} collective-permute-done((f32[136,2048]{1,0:T(8,128)S(1)}, f32[136,2048]{1,0:T(8,128)}, u32[]{:S(2)}, u32[]{:S(2)}) %collective-permute-start.1) | collective-permute-done | bytes 1114144 | tf_op jit(solution)/shard_map/ppermute | solution.py:69
  40.4 1.6 select_select_fusion
  42.0 1.9 %collective-permute-start.4 = (f32[136,2048]{1,0:T(8,128)S(1)}, f32[136,2048]{1,0:T(8,128)S(1)}, u32[]{:S(2)}, u32[]{:S(2)}) collective-permute-start(f32[136,2048]{1,0:T(8,128)S(1)} %select_select_fusion), channel_id=1, source_target_pairs={{32,48},{48,32},{64,80},{80,64},{96,112},{112,96},{33,49},{49,33},... | collective-permute-start | bytes 3342344 | tf_op jit(solution)/shard_map/ppermute | solution.py:78
  44.1 2.5 %collective-permute-done.4 = f32[136,2048]{1,0:T(8,128)S(1)} collective-permute-done((f32[136,2048]{1,0:T(8,128)S(1)}, f32[136,2048]{1,0:T(8,128)S(1)}, u32[]{:S(2)}, u32[]{:S(2)}) %collective-permute-start.4) | collective-permute-done | bytes 1114144 | tf_op jit(solution)/shard_map/ppermute | solution.py:78
  48.3 1.9 fusion.6
  50.1 3.3 %collective-permute-start.10 = (f32[256,256]{0,1:T(8,128)S(1)}, f32[256,256]{0,1:T(8,128)S(1)}, u32[]{:S(2)}, u32[]{:S(2)}) collective-permute-start(f32[256,256]{0,1:T(8,128)S(1)} %fusion.6), channel_id=1, source_target_pairs={{0,2},{1,3},{2,0},{3,1},{4,6},{5,7},{6,4},{7,5},{8,10},{9,11},{10,... | collective-permute-start | bytes 786440 | tf_op jit(solution)/shard_map/ppermute | solution.py:56
  53.4 1.1 collective-permute-start.11
  54.5 36.7 %fusion.3 = f32[2944,256]{0,1:T(8,128)S(1)} fusion(f32[368,8,16,128]{3,2,1,0:T(8,128)} %bitcast.112, f32[128,2048]{1,0:T(8,128)S(1)} %slice.204, f32[128,2048]{1,0:T(8,128)S(1)} %slice.203), kind=kOutput, calls=%fused_computation.3 | convolution fusion | flops 18522570752 | bytes 29229056 | tf_op jit(solution)/shard_map/dot_general | solution.py:34
  91.2 2.3 %copy.28 = f32[2944,256]{1,0:T(8,128)} copy(f32[2944,256]{0,1:T(8,128)S(1)} %fusion.3) | data formatting | bytes 6029312 | tf_op jit(solution)/shard_map/dot_general | solution.py:34
  93.5 2.6 %dynamic-slice_bitcast_fusion = f32[2,2,2,184,256]{4,3,2,1,0:T(8,128)} fusion(f32[2,2,2,2,184,256]{5,4,3,2,1,0:T(8,128)} %bitcast.116, s32[]{:T(128)S(6)} %select_n.208), kind=kLoop, calls=%fused_computation.7 | loop fusion | bytes 3014660 | tf_op jit(solution)/shard_map/jit(dynamic_index_in_dim)/squeeze | solution.py:93
  96.1 2.0 %collective-permute-start.5 = (f32[2,2,2,184,256]{4,3,2,1,0:T(8,128)}, f32[2,2,2,184,256]{4,3,2,1,0:T(8,128)}, u32[]{:S(2)}, u32[]{:S(2)}) collective-permute-start(f32[2,2,2,184,256]{4,3,2,1,0:T(8,128)} %dynamic-slice_bitcast_fusion), channel_id=1, source_target_pairs={{0,1},{1,0},{2,3},{3,2},{4,5},{5,4},{6,7},{7,6},{8,9},{9,8},{10,11... | collective-permute-start | bytes 4521992 | tf_op jit(solution)/shard_map/ppermute | solution.py:94
  98.9 1.3 add_add_fusion.1
  100.2 2.0 %collective-permute-start.12 = (f32[256,256]{0,1:T(8,128)S(1)}, f32[256,256]{0,1:T(8,128)S(1)}, u32[]{:S(2)}, u32[]{:S(2)}) collective-permute-start(f32[256,256]{0,1:T(8,128)S(1)} %add_add_fusion.1), channel_id=1, source_target_pairs={{0,4},{1,5},{2,6},{3,7},{4,0},{5,1},{6,2},{7,3},{8,12},{9,13},{10,... | collective-permute-start | bytes 786440 | tf_op jit(solution)/shard_map/ppermute | solution.py:56
  102.2 3.6 %collective-permute-start.13 = (f32[256,256]{0,1:T(8,128)S(1)}, f32[256,256]{0,1:T(8,128)}, u32[]{:S(2)}, u32[]{:S(2)}) collective-permute-start(f32[256,256]{0,1:T(8,128)S(1)} %add_add_fusion.1), channel_id=1, source_target_pairs={{0,8},{1,9},{2,10},{3,11},{4,12},{5,13},{6,14},{7,15},{8,0},{9,1},... | collective-permute-start | bytes 786440 | tf_op jit(solution)/shard_map/ppermute | solution.py:56
  107.8 1.4 slice_bitcast_fusion
  109.5 7.3 %collective-permute-done.13 = f32[256,256]{0,1:T(8,128)} collective-permute-done((f32[256,256]{0,1:T(8,128)S(1)}, f32[256,256]{0,1:T(8,128)}, u32[]{:S(2)}, u32[]{:S(2)}) %collective-permute-start.13) | collective-permute-done | bytes 262176 | tf_op jit(solution)/shard_map/ppermute | solution.py:56
  116.8 2.6 %collective-permute-done.14 = f32[256,256]{0,1:T(8,128)} collective-permute-done((f32[256,256]{0,1:T(8,128)S(1)}, f32[256,256]{0,1:T(8,128)}, u32[]{:S(2)}, u32[]{:S(2)}) %collective-permute-start.14) | collective-permute-done | bytes 262176 | tf_op jit(solution)/shard_map/ppermute | solution.py:56
  119.4 1.2 add_add_fusion
  121.0 11.7 %cholesky.44 = f32[128,128]{1,0:T(8,128)S(1)} custom-call(f32[128,128]{1,0:T(8,128)S(1)} %fusion.25), custom_call_target="Cholesky" | custom-call | tf_op jit(solution)/shard_map/jit(cholesky)/cholesky | solution.py:44
  134.1 9.8 %custom-call.6 = f32[1,128,128]{1,2,0:T(8,128)S(1)} custom-call(f32[1,128,128]{2,1,0:T(8,128)S(1)} %fusion.12), custom_call_target="InvertDiagBlocksLowerTriangular" | custom-call | tf_op jit(solution)/shard_map/jit(_solve_triangular)/triangular_solve | solution.py:45
  143.9 1.6 bitcast_add_fusion
  145.5 1.1 copy-done.1
  148.1 11.7 %cholesky.55 = f32[128,128]{1,0:T(8,128)S(1)} custom-call(f32[128,128]{1,0:T(8,128)S(1)} %fusion.23), custom_call_target="Cholesky" | custom-call | tf_op jit(solution)/shard_map/jit(cholesky)/cholesky | solution.py:44
  159.8 4.1 %collective-permute-done.6 = f32[2,2,184,256]{3,2,1,0:T(8,128)S(1)} collective-permute-done((f32[2,2,184,256]{3,2,1,0:T(8,128)S(1)}, f32[2,2,184,256]{3,2,1,0:T(8,128)S(1)}, u32[]{:S(2)}, u32[]{:S(2)}) %collective-permute-start.6) | collective-permute-done | bytes 753696 | tf_op jit(solution)/shard_map/ppermute | solution.py:94
  163.9 1.2 bitcast_add_fusion.1
  165.4 2.2 %collective-permute-start.7 = (f32[2,184,256]{1,2,0:T(8,128)S(1)}, f32[2,184,256]{1,2,0:T(8,128)S(1)}, u32[]{:S(2)}, u32[]{:S(2)}) collective-permute-start(f32[2,184,256]{1,2,0:T(8,128)S(1)} %bitcast.119), channel_id=1, source_target_pairs={{0,2},{1,3},{2,0},{3,1},{4,6},{5,7},{6,4},{7,5},{8,10},{9,11},{10,... | collective-permute-start | bytes 1130504 | tf_op jit(solution)/shard_map/ppermute | solution.py:94
  168.9 9.8 %custom-call.7 = f32[1,128,128]{1,2,0:T(8,128)S(1)} custom-call(f32[1,128,128]{2,1,0:T(8,128)S(1)} %fusion.13), custom_call_target="InvertDiagBlocksLowerTriangular" | custom-call | tf_op jit(solution)/shard_map/jit(_solve_triangular)/triangular_solve | solution.py:45
  180.4 6.6 %collective-permute-done.8 = f32[184,256]{0,1:T(8,128)S(1)} collective-permute-done((f32[184,256]{0,1:T(8,128)S(1)}, f32[184,256]{0,1:T(8,128)S(1)}, u32[]{:S(2)}, u32[]{:S(2)}) %collective-permute-start.8) | collective-permute-done | bytes 188448 | tf_op jit(solution)/shard_map/ppermute | solution.py:94
  (94 shorter events, 17.7 us)
Async XLA Ops:
  5.8 1.0 copy-start.5
  5.8 0.8 collective-permute-start
  7.9 3.7 %collective-permute-start.2 = (f32[136,2048]{1,0:T(8,128)}, f32[136,2048]{1,0:T(8,128)S(1)}, u32[]{:S(2)}, u32[]{:S(2)}) collective-permute-start(f32[136,2048]{1,0:T(8,128)} %broadcast_select_fusion.1), channel_id=1, source_target_pairs={{16,48},{0,96},{17,49},{1,97},{18,50},{2,98},{19,51},{3,99},{20,52... | collective-permute-start | bytes 3342344 | tf_op jit(solution)/shard_map/ppermute | solution.py:70
  8.6 31.8 %collective-permute-start.1 = (f32[136,2048]{1,0:T(8,128)S(1)}, f32[136,2048]{1,0:T(8,128)}, u32[]{:S(2)}, u32[]{:S(2)}) collective-permute-start(f32[136,2048]{1,0:T(8,128)S(1)} %collective-permute-done), channel_id=1, source_target_pairs={{32,64},{112,80},{33,65},{113,81},{34,66},{114,82},{35,67},{115,83... | collective-permute-start | bytes 3342344 | tf_op jit(solution)/shard_map/ppermute | solution.py:69
  9.9 34.2 %collective-permute-start.3 = (f32[136,2048]{1,0:T(8,128)}, f32[136,2048]{1,0:T(8,128)}, u32[]{:S(2)}, u32[]{:S(2)}) collective-permute-start(f32[136,2048]{1,0:T(8,128)} %copy-done.5), channel_id=1, source_target_pairs={{0,16},{16,0},{1,17},{17,1},{2,18},{18,2},{3,19},{19,3},{4,20},{20... | collective-permute-start | bytes 3342344 | tf_op jit(solution)/shard_map/ppermute | solution.py:67
  11.6 32.3 %copy-start.8 = (s32[23,1,128]{2,1,0:T(1,128)S(1)}, s32[23,1,128]{2,1,0:T(1,128)}, u32[]{:S(2)}) copy-start(s32[23,1,128]{2,1,0:T(1,128)} %param.13) | copy-start | bytes 35332
  11.6 1.0 copy-start.4
  42.0 4.6 %collective-permute-start.4 = (f32[136,2048]{1,0:T(8,128)S(1)}, f32[136,2048]{1,0:T(8,128)S(1)}, u32[]{:S(2)}, u32[]{:S(2)}) collective-permute-start(f32[136,2048]{1,0:T(8,128)S(1)} %select_select_fusion), channel_id=1, source_target_pairs={{32,48},{48,32},{64,80},{80,64},{96,112},{112,96},{33,49},{49,33},... | collective-permute-start | bytes 3342344 | tf_op jit(solution)/shard_map/ppermute | solution.py:78
  46.9 1.0 copy-start.2
  46.9 1.4 copy-start.3
  50.1 48.0 %collective-permute-start.10 = (f32[256,256]{0,1:T(8,128)S(1)}, f32[256,256]{0,1:T(8,128)S(1)}, u32[]{:S(2)}, u32[]{:S(2)}) collective-permute-start(f32[256,256]{0,1:T(8,128)S(1)} %fusion.6), channel_id=1, source_target_pairs={{0,2},{1,3},{2,0},{3,1},{4,6},{5,7},{6,4},{7,5},{8,10},{9,11},{10,... | collective-permute-start | bytes 786440 | tf_op jit(solution)/shard_map/ppermute | solution.py:56
  53.4 44.8 %collective-permute-start.11 = (f32[256,256]{0,1:T(8,128)S(1)}, f32[256,256]{0,1:T(8,128)}, u32[]{:S(2)}, u32[]{:S(2)}) collective-permute-start(f32[256,256]{0,1:T(8,128)S(1)} %fusion.6), channel_id=1, source_target_pairs={{0,3},{1,2},{2,1},{3,0},{4,7},{5,6},{6,5},{7,4},{8,11},{9,10},{10,... | collective-permute-start | bytes 786440 | tf_op jit(solution)/shard_map/ppermute | solution.py:56
  54.4 44.4 %collective-permute-start.9 = (f32[256,256]{0,1:T(8,128)S(1)}, f32[256,256]{0,1:T(8,128)}, u32[]{:S(2)}, u32[]{:S(2)}) collective-permute-start(f32[256,256]{0,1:T(8,128)S(1)} %fusion.6), channel_id=1, source_target_pairs={{0,1},{1,0},{2,3},{3,2},{4,5},{5,4},{6,7},{7,6},{8,9},{9,8},{10,11... | collective-permute-start | bytes 786440 | tf_op jit(solution)/shard_map/ppermute | solution.py:56
  96.1 47.8 %collective-permute-start.5 = (f32[2,2,2,184,256]{4,3,2,1,0:T(8,128)}, f32[2,2,2,184,256]{4,3,2,1,0:T(8,128)}, u32[]{:S(2)}, u32[]{:S(2)}) collective-permute-start(f32[2,2,2,184,256]{4,3,2,1,0:T(8,128)} %dynamic-slice_bitcast_fusion), channel_id=1, source_target_pairs={{0,1},{1,0},{2,3},{3,2},{4,5},{5,4},{6,7},{7,6},{8,9},{9,8},{10,11... | collective-permute-start | bytes 4521992 | tf_op jit(solution)/shard_map/ppermute | solution.py:94
  98.1 0.7 copy-start.7
  98.9 45.0 %copy-start = (f32[2944,256]{1,0:T(8,128)S(1)}, f32[2944,256]{1,0:T(8,128)}, u32[]{:S(2)}) copy-start(f32[2944,256]{1,0:T(8,128)} %copy.28) | copy-start | bytes 9043972
  100.2 9.3 %collective-permute-start.12 = (f32[256,256]{0,1:T(8,128)S(1)}, f32[256,256]{0,1:T(8,128)S(1)}, u32[]{:S(2)}, u32[]{:S(2)}) collective-permute-start(f32[256,256]{0,1:T(8,128)S(1)} %add_add_fusion.1), channel_id=1, source_target_pairs={{0,4},{1,5},{2,6},{3,7},{4,0},{5,1},{6,2},{7,3},{8,12},{9,13},{10,... | collective-permute-start | bytes 786440 | tf_op jit(solution)/shard_map/ppermute | solution.py:56
  102.2 14.6 %collective-permute-start.13 = (f32[256,256]{0,1:T(8,128)S(1)}, f32[256,256]{0,1:T(8,128)}, u32[]{:S(2)}, u32[]{:S(2)}) collective-permute-start(f32[256,256]{0,1:T(8,128)S(1)} %add_add_fusion.1), channel_id=1, source_target_pairs={{0,8},{1,9},{2,10},{3,11},{4,12},{5,13},{6,14},{7,15},{8,0},{9,1},... | collective-permute-start | bytes 786440 | tf_op jit(solution)/shard_map/ppermute | solution.py:56
  105.8 13.6 %collective-permute-start.14 = (f32[256,256]{0,1:T(8,128)S(1)}, f32[256,256]{0,1:T(8,128)}, u32[]{:S(2)}, u32[]{:S(2)}) collective-permute-start(f32[256,256]{0,1:T(8,128)S(1)} %add_add_fusion.1), channel_id=1, source_target_pairs={{0,12},{1,13},{2,14},{3,15},{4,8},{5,9},{6,10},{7,11},{8,4},{9,5},... | collective-permute-start | bytes 786440 | tf_op jit(solution)/shard_map/ppermute | solution.py:56
  109.5 7.3 %copy-start.6 = (f32[256,256]{0,1:T(8,128)}, f32[256,256]{0,1:T(8,128)S(1)}, u32[]{:S(2)}) copy-start(f32[256,256]{0,1:T(8,128)S(1)} %collective-permute-done.12) | copy-start | bytes 786436
  145.5 1.1 copy-start.1
  146.6 0.6 copy-start.13
  146.6 0.6 copy-start.14
  146.6 0.6 copy-start.15
  146.6 1.0 copy-start.16
  146.7 17.2 %collective-permute-start.6 = (f32[2,2,184,256]{3,2,1,0:T(8,128)S(1)}, f32[2,2,184,256]{3,2,1,0:T(8,128)S(1)}, u32[]{:S(2)}, u32[]{:S(2)}) collective-permute-start(f32[2,2,184,256]{3,2,1,0:T(8,128)S(1)} %dynamic-slice_bitcast_fusion.1), channel_id=1, source_target_pairs={{0,4},{1,5},{2,6},{3,7},{4,0},{5,1},{6,2},{7,3},{8,12},{9,13},{10,... | collective-permute-start | bytes 2261000 | tf_op jit(solution)/shard_map/ppermute | solution.py:94
  165.4 13.5 %collective-permute-start.7 = (f32[2,184,256]{1,2,0:T(8,128)S(1)}, f32[2,184,256]{1,2,0:T(8,128)S(1)}, u32[]{:S(2)}, u32[]{:S(2)}) collective-permute-start(f32[2,184,256]{1,2,0:T(8,128)S(1)} %bitcast.119), channel_id=1, source_target_pairs={{0,2},{1,3},{2,0},{3,1},{4,6},{5,7},{6,4},{7,5},{8,10},{9,11},{10,... | collective-permute-start | bytes 1130504 | tf_op jit(solution)/shard_map/ppermute | solution.py:94
  179.0 8.1 %copy-start.9 = (f32[1,184]{1,0:T(1,128)S(1)}, f32[1,184]{1,0:T(1,128)}, u32[]{:S(2)}) copy-start(f32[1,184]{1,0:T(1,128)} %get-tuple-element.61) | copy-start | bytes 2212
  179.0 8.1 %copy-start.10 = (f32[1,184]{1,0:T(1,128)S(1)}, f32[1,184]{1,0:T(1,128)}, u32[]{:S(2)}) copy-start(f32[1,184]{1,0:T(1,128)} %get-tuple-element.62) | copy-start | bytes 2212
  179.0 8.1 %copy-start.11 = (f32[1,184]{1,0:T(1,128)S(1)}, f32[1,184]{1,0:T(1,128)}, u32[]{:S(2)}) copy-start(f32[1,184]{1,0:T(1,128)} %get-tuple-element.63) | copy-start | bytes 2212
  179.0 8.3 %copy-start.12 = (f32[128]{0:T(128)S(1)}, f32[128]{0:T(128)}, u32[]{:S(2)}) copy-start(f32[128]{0:T(128)} %slice.189) | copy-start | bytes 1540
  179.1 8.0 %collective-permute-start.8 = (f32[184,256]{0,1:T(8,128)S(1)}, f32[184,256]{0,1:T(8,128)S(1)}, u32[]{:S(2)}, u32[]{:S(2)}) collective-permute-start(f32[184,256]{0,1:T(8,128)S(1)} %dynamic-slice_bitcast_fusion.2), channel_id=1, source_target_pairs={{0,8},{1,9},{2,10},{3,11},{4,12},{5,13},{6,14},{7,15},{8,0},{9,1},... | collective-permute-start | bytes 565256 | tf_op jit(solution)/shard_map/ppermute | solution.py:94
